TPU v7x, 128 devices: a whole 4x4x4 slice. The times are simulated.
128 devices in a mesh: enc: 16 (over z, y), dp: 2 (over x_hi), tensor: 4 (over x_lo, core).
Axes of the slice: x: 4 (x_hi: 2, x_lo: 2; x = x_hi * 2 + x_lo), y: 4, z: 4, core: 2. Of those that a mesh axis runs over, the one named last changes fastest.
Arguments:
- hidden_in: bfloat16 [3, 64, 4096], P(None, 'dp', 'enc')
- self_cache: bfloat16 [64, 8, 2, 2048], P(('dp', 'enc'), None, None, 'tensor'), may hold values from -6 to 6
- src_pool: bfloat16 [64, 24, 2, 2048], P(('dp', 'enc'), None, None, 'tensor'), may hold values from -6 to 6
- assign: int32 [64], replicated, may hold values from 0 to 63, as said below
- src_len: int32 [64], replicated, may hold values from 1 to 24, 768 in all
- positions: int32 [64], replicated, may hold values from 1 to 8, 256 in all
- gain_self: float32 [4096], P('enc'), may hold values from 0.1 to 1.9
- w_qkv: bfloat16 [4096, 3, 2048], P('enc', None, 'tensor'), may hold values from -0.09375 to 0.09375
- w_out_self: bfloat16 [2048, 4096], P('tensor', 'enc'), may hold values from -0.125 to 0.125
- gain_cross: float32 [4096], P('enc'), may hold values from 0.1 to 1.9
- w_q_cross: bfloat16 [4096, 2048], P('enc', 'tensor'), may hold values from -0.09375 to 0.09375
- w_out_cross: bfloat16 [2048, 4096], P('tensor', 'enc'), may hold values from -0.125 to 0.125
Outputs:
- layer_out: bfloat16 [3, 64, 4096], P(None, 'dp', 'enc')
Inputs may be any that keep to these rules, and one draw needn't show every extreme that they name: `assign`: a permutation of the 64 sources; with blocks of 2 consecutive sequences or sources numbered d * 16 + e, the 2 sequences of block d * 16 + e read exactly one source from each block d2 * 16 + e that has the same e.
All inputs are finite; a program needn't handle non-finite values.
Results may differ from a plain program's by a relative error of at most 0.008.
Values may be sent and summed in bfloat16 or wider, within the bound.
No kernel may reach another device: no remote copies, remote signals or barrier semaphores. Data moves between devices by JAX's collectives and lax.ppermute only.
A program may use at most 64 MiB of HBM per device.

v0:
```python
import math
import jax
import jax.numpy as jnp
from jax import lax
from jax.sharding import PartitionSpec as P

D = 4096
DK = 256
STEPS = 3
EPSILON = 1e-06


def row_norm(rows_in, gain_vec):
    squares = lax.psum(jnp.sum(rows_in * rows_in, axis=1), "enc")
    return (rows_in * lax.rsqrt(squares / D + EPSILON)[:, None] * gain_vec[None, :]).astype(
        jnp.bfloat16
    )


def score_weight(scores):
    return jnp.exp(scores).astype(jnp.bfloat16)


def attend(query_rows, key_rows, value_rows, usable):
    count = query_rows.shape[0]
    head_count = query_rows.shape[1] // DK
    query_heads = query_rows.reshape(count, head_count, DK)
    key_heads = key_rows.reshape(count, key_rows.shape[1], head_count, DK)
    value_heads = value_rows.reshape(count, value_rows.shape[1], head_count, DK)
    scores = jnp.einsum(
        "nhd,nlhd->nhl", query_heads, key_heads, preferred_element_type=jnp.float32
    ) * (1.0 / math.sqrt(DK))
    weights = jnp.where(usable[:, None, :], score_weight(scores), jnp.zeros((), jnp.bfloat16))
    weighted = jnp.einsum("nhl,nlhd->nhd", weights, value_heads, preferred_element_type=jnp.float32)
    return (weighted, jnp.sum(weights.astype(jnp.float32), axis=-1))


def combine_heads(context, weight_out):
    partial_out = jnp.dot(context, weight_out, preferred_element_type=jnp.float32)
    return lax.psum(partial_out, "tensor")


def on_device(
    hidden_in,
    self_cache,
    src_pool,
    assign,
    src_len,
    positions,
    gain_self,
    w_qkv,
    w_out_self,
    gain_cross,
    w_q_cross,
    w_out_cross,
):
    dp_count = lax.axis_size("dp")
    enc_count = lax.axis_size("enc")
    seq_dev = self_cache.shape[0]
    per_pair = seq_dev // dp_count
    cache_len = self_cache.shape[1]
    source_len = src_pool.shape[1]
    enc_at = lax.axis_index("enc")
    dp_at = lax.axis_index("dp")
    block_at = dp_at * enc_count + enc_at
    slot_index = jnp.arange(seq_dev, dtype=jnp.int32)
    my_slots = block_at * seq_dev + slot_index
    my_positions = jnp.take(positions, my_slots)
    my_sources = jnp.take(assign, my_slots)
    place_at = jnp.arange(cache_len, dtype=jnp.int32)
    cache_usable = place_at[None, :] < my_positions[:, None]
    token_at = jnp.arange(source_len, dtype=jnp.int32)
    assign_view = assign.reshape(dp_count, enc_count, seq_dev)
    assign_grid = jnp.take(assign_view, enc_at, axis=1)
    owners = assign_grid // (seq_dev * enc_count)
    earlier = (owners[:, None, :] == owners[:, :, None]) & (
        slot_index[None, None, :] < slot_index[None, :, None]
    )
    slot_rank = jnp.sum(earlier.astype(jnp.int32), axis=2)
    recv_rows = jnp.take(owners, dp_at, axis=0) * per_pair + jnp.take(slot_rank, dp_at, axis=0)
    picked = (owners == dp_at)[:, :, None] & (
        slot_rank[:, :, None] == jnp.arange(per_pair, dtype=jnp.int32)[None, None, :]
    )
    chosen = jnp.sum(jnp.where(picked, (assign_grid % seq_dev)[:, :, None], 0), axis=1)
    chosen_flat = chosen.reshape(-1)
    outgoing = jnp.take(src_pool, chosen_flat, axis=0)
    arrived = lax.all_to_all(outgoing, "dp", split_axis=0, concat_axis=0, tiled=True)
    cross_kv = jnp.take(arrived, recv_rows, axis=0)
    cross_usable = token_at[None, :] < jnp.take(src_len, my_sources)[:, None]
    key_list = []
    value_list = []
    results = []
    for step_at in range(STEPS):
        current = hidden_in[step_at].astype(jnp.float32)
        normed = row_norm(current, gain_self)
        projected = jnp.einsum("sd,dcw->scw", normed, w_qkv, preferred_element_type=jnp.float32)
        own_proj = lax.psum_scatter(projected, "enc", scatter_dimension=0, tiled=True).astype(
            jnp.bfloat16
        )
        query_rows = own_proj[:, 0]
        key_list.append(own_proj[:, 1])
        value_list.append(own_proj[:, 2])
        weighted, totals = attend(
            query_rows, self_cache[:, :, 0], self_cache[:, :, 1], cache_usable
        )
        head_count = weighted.shape[1]
        query_heads = query_rows.astype(jnp.float32).reshape(seq_dev, head_count, DK)
        for key_new, value_new in zip(key_list, value_list):
            scores = jnp.sum(
                query_heads * key_new.astype(jnp.float32).reshape(seq_dev, head_count, DK), axis=-1
            ) * (1.0 / math.sqrt(DK))
            weights = score_weight(scores).astype(jnp.float32)
            weighted = weighted + weights[:, :, None] * value_new.astype(jnp.float32).reshape(
                seq_dev, head_count, DK
            )
            totals = totals + weights
        context = (
            (weighted / totals[:, :, None]).reshape(seq_dev, head_count * DK).astype(jnp.bfloat16)
        )
        context_all = lax.all_gather(context, "enc", axis=0, tiled=True)
        residual = current + combine_heads(context_all, w_out_self)
        normed_cross = row_norm(residual, gain_cross)
        cross_query = jnp.dot(normed_cross, w_q_cross, preferred_element_type=jnp.float32)
        own_query = lax.psum_scatter(cross_query, "enc", scatter_dimension=0, tiled=True).astype(
            jnp.bfloat16
        )
        weighted, totals = attend(own_query, cross_kv[:, :, 0], cross_kv[:, :, 1], cross_usable)
        context = (
            (weighted / totals[:, :, None]).reshape(seq_dev, head_count * DK).astype(jnp.bfloat16)
        )
        context_all = lax.all_gather(context, "enc", axis=0, tiled=True)
        output_rows = residual + combine_heads(context_all, w_out_cross)
        results.append(output_rows.astype(jnp.bfloat16))
    return jnp.stack(results)


def solution(mesh):
    in_specs = (
        P(None, "dp", "enc"),
        P(("dp", "enc"), None, None, "tensor"),
        P(("dp", "enc"), None, None, "tensor"),
        P(),
        P(),
        P(),
        P("enc"),
        P("enc", None, "tensor"),
        P("tensor", "enc"),
        P("enc"),
        P("enc", "tensor"),
        P("tensor", "enc"),
    )
    out_specs = P(None, "dp", "enc")
    return jax.shard_map(
        on_device, mesh=mesh, in_specs=in_specs, out_specs=out_specs, check_vma=False
    )
```

profile of v0, /device:TPU:1, one launch (start us, length us, event | category | flops | bytes accessed | tf_op | source)
XLA Modules:
  0.0 470.3 jit_solution(5215867503166297110)
XLA Ops:
  6.6 0.7 copy-done.1
  7.4 0.2 fusion.80
  7.8 0.6 gather_fusion.1
  8.5 0.2 copy-done.12
  8.7 0.7 gather_fusion.3
  9.4 0.8 broadcast_select_fusion.1
  10.2 5.0 %all-to-all-start = ((bf16[2,24,2,512]{3,2,1,0:T(2,128)(2,1)}), bf16[2,24,2,512]{3,2,1,0:T(2,128)(2,1)S(1)}, u32[]{:S(2)}, u32[]{:S(2)}) async-start(bf16[2,24,2,512]{3,2,1,0:T(2,128)(2,1)} %broadcast_select_fusion.1), calls=%async_computation | async-start | bytes 196608 | tf_op jit(solution)/shard_map/all_to_all | solution.py:87
  15.3 34.7 %all-reduce.9 = (f32[32]{0:T(128)S(1)}, f32[32]{0:T(128)S(1)}, f32[32]{0:T(128)S(1)}) all-reduce(f32[32]{0:T(128)S(1)} %get-tuple-element.35, f32[32]{0:T(128)S(1)} %get-tuple-element.36, f32[32]{0:T(128)S(1)} %get-tuple-element.37), channel_id=1, replica_groups=mesh['enc'=16,'dp'=2,'tensor'=4] {'enc'}, use_global_device_ids=true, to_apply=%region_1.3 | all-reduce | flops 96 | bytes 768 | tf_op jit(solution)/shard_map/psum | solution.py:14
  50.0 0.7 copy-done.14
  50.7 0.3 fusion.34
  51.0 0.3 fusion.37
  51.3 0.3 fusion.40
  51.6 0.7 copy-done.15
  52.2 0.6 dynamic-slice.11
  53.5 62.2 %all-reduce.20 = (bf16[32,3,512]{2,0,1:T(8,128)(2,1)S(1)}, bf16[32,3,512]{2,0,1:T(8,128)(2,1)S(1)}, bf16[32,3,512]{2,0,1:T(8,128)(2,1)S(1)}) all-reduce(f32[32,3,512]{2,0,1:T(8,128)S(1)} %fusion.40, f32[32,3,512]{2,0,1:T(8,128)S(1)} %fusion.34, f32[32,3,512]{2,0,1:T(8,128)S(1)} %fusion.37), channel_id=2, replica_groups=mesh['enc'=16,'dp'=2,'tensor'=4] {'enc'}, use_global_device_ids=true, to_apply=%region_2.4.clone | all-reduce | flops 147456 | bytes 884736
  116.0 0.6 copy-done.11
  117.1 0.4 copy-done.2
  117.5 0.6 gather_fusion
  119.0 15.2 %all-gather = bf16[16,2,512]{2,1,0:T(2,128)(2,1)S(1)} all-gather(bf16[1,2,512]{2,1,0:T(2,128)(2,1)S(1)} %reshape.380), channel_id=1, replica_groups=mesh['enc'=16,'dp'=2,'tensor'=4] {'enc'}, dimensions={0}, use_global_device_ids=true | all-gather | bytes 34816 | tf_op jit(solution)/shard_map/all_gather | solution.py:120
  134.2 18.0 %all-gather.2 = bf16[16,2,512]{2,1,0:T(2,128)(2,1)S(1)} all-gather(bf16[1,2,512]{2,1,0:T(2,128)(2,1)S(1)} %reshape.384), channel_id=1, replica_groups=mesh['enc'=16,'dp'=2,'tensor'=4] {'enc'}, dimensions={0}, use_global_device_ids=true | all-gather | bytes 34816 | tf_op jit(solution)/shard_map/all_gather | solution.py:120
  152.3 0.8 fusion.102
  153.1 0.8 fusion.105
  153.8 15.4 %all-gather.4 = bf16[16,2,512]{2,1,0:T(2,128)(2,1)S(1)} all-gather(bf16[1,2,512]{2,1,0:T(2,128)(2,1)S(1)} %reshape.388), channel_id=1, replica_groups=mesh['enc'=16,'dp'=2,'tensor'=4] {'enc'}, dimensions={0}, use_global_device_ids=true | all-gather | bytes 34816 | tf_op jit(solution)/shard_map/all_gather | solution.py:120
  169.3 0.8 fusion.108
  170.1 0.5 copy-done.3
  170.7 0.6 gather_fusion.2
  171.4 0.7 gather_fusion.4
  172.2 0.2 broadcast_select_fusion
  172.3 0.4 slice_reduce_fusion.1
  172.8 70.9 %all-reduce.19.cloned.1.call-done = (f32[32,256]{1,0:T(8,128)}, f32[32,256]{1,0:T(8,128)}, f32[32,256]{1,0:T(8,128)}) async-done(((f32[32,256]{1,0:T(8,128)}, f32[32,256]{1,0:T(8,128)}, f32[32,256]{1,0:T(8,128)}), (f32[32,256]{1,0:T(8,128)}, f32[32,256]{1,0:T(8,128)}, f32[32,256]{1,0:T(8,128)})) %all-reduce.19.cloned.1.call-update) | async-done | bytes 98320 | tf_op jit(solution)/shard_map/psum | solution.py:40
  243.7 1.0 multiply_reduce_fusion.2
  244.6 33.3 %all-reduce.7 = (f32[32]{0:T(128)S(1)}, f32[32]{0:T(128)S(1)}, f32[32]{0:T(128)S(1)}) all-reduce(f32[32]{0:T(128)S(1)} %get-tuple-element.34, f32[32]{0:T(128)S(1)} %get-tuple-element.33, f32[32]{0:T(128)S(1)} %get-tuple-element.32), channel_id=1, replica_groups=mesh['enc'=16,'dp'=2,'tensor'=4] {'enc'}, use_global_device_ids=true, to_apply=%region_34.38 | all-reduce | flops 96 | bytes 768 | tf_op jit(solution)/shard_map/psum | solution.py:14
  278.0 0.7 copy-done.13
  278.7 0.2 fusion.27
  278.9 0.6 copy-done.9
  279.4 0.2 fusion.29
  279.6 0.6 copy-done.10
  280.2 0.2 fusion.31
  280.4 57.3 %all-reduce.21 = (bf16[32,512]{1,0:T(8,128)(2,1)S(1)}, bf16[32,512]{1,0:T(8,128)(2,1)S(1)}, bf16[32,512]{1,0:T(8,128)(2,1)S(1)}) all-reduce(f32[32,512]{1,0:T(8,128)S(1)} %fusion.31, f32[32,512]{1,0:T(8,128)S(1)} %fusion.29, f32[32,512]{1,0:T(8,128)S(1)} %fusion.27), channel_id=7, replica_groups=mesh['enc'=16,'dp'=2,'tensor'=4] {'enc'}, use_global_device_ids=true, to_apply=%region_35.39.clone | all-reduce | flops 49152 | bytes 294912
  338.5 16.3 %all-gather.1 = bf16[16,2,512]{2,1,0:T(2,128)(2,1)S(1)} all-gather(bf16[1,2,512]{2,1,0:T(2,128)(2,1)S(1)} %reshape.382), channel_id=1, replica_groups=mesh['enc'=16,'dp'=2,'tensor'=4] {'enc'}, dimensions={0}, use_global_device_ids=true | all-gather | bytes 34816 | tf_op jit(solution)/shard_map/all_gather | solution.py:131
  355.0 17.4 %all-gather.3 = bf16[16,2,512]{2,1,0:T(2,128)(2,1)S(1)} all-gather(bf16[1,2,512]{2,1,0:T(2,128)(2,1)S(1)} %reshape.386), channel_id=1, replica_groups=mesh['enc'=16,'dp'=2,'tensor'=4] {'enc'}, dimensions={0}, use_global_device_ids=true | all-gather | bytes 34816 | tf_op jit(solution)/shard_map/all_gather | solution.py:131
  372.5 0.8 fusion.103
  373.2 0.8 fusion.106
  374.2 15.7 %all-gather.5 = bf16[16,2,512]{2,1,0:T(2,128)(2,1)S(1)} all-gather(bf16[1,2,512]{2,1,0:T(2,128)(2,1)S(1)} %reshape.390), channel_id=1, replica_groups=mesh['enc'=16,'dp'=2,'tensor'=4] {'enc'}, dimensions={0}, use_global_device_ids=true | all-gather | bytes 34816 | tf_op jit(solution)/shard_map/all_gather | solution.py:131
  389.9 0.8 fusion.109
  390.7 71.3 %all-reduce.17.cloned.1.call-done = (f32[32,256]{1,0:T(8,128)}, f32[32,256]{1,0:T(8,128)}, f32[32,256]{1,0:T(8,128)}) async-done(((f32[32,256]{1,0:T(8,128)}, f32[32,256]{1,0:T(8,128)}, f32[32,256]{1,0:T(8,128)}), (f32[32,256]{1,0:T(8,128)}, f32[32,256]{1,0:T(8,128)}, f32[32,256]{1,0:T(8,128)})) %all-reduce.17.cloned.1.call-update) | async-done | bytes 98320 | tf_op jit(solution)/shard_map/psum | solution.py:40
  462.1 0.8 fusion.28
  462.9 0.6 pad_maximum_fusion
  (109 shorter events, 3.5 us)
Async XLA Ops:
  6.5 43.5 %copy-start = (bf16[256,3,512]{2,0,1:T(8,128)(2,1)S(1)}, bf16[256,3,512]{2,0,1:T(8,128)(2,1)}, u32[]{:S(2)}) copy-start(bf16[256,3,512]{2,0,1:T(8,128)(2,1)} %param.25) | copy-start | bytes 2359300
  6.6 0.7 copy-start.1
  7.8 0.9 copy-start.12
  10.2 5.0 %copy-start.7 = (bf16[3,32,256]{2,1,0:T(8,128)(2,1)S(1)}, bf16[3,32,256]{2,1,0:T(8,128)(2,1)}, u32[]{:S(2)}) copy-start(bf16[3,32,256]{2,1,0:T(8,128)(2,1)} %param.18) | copy-start | bytes 147460
  10.2 161.2 %all-to-all-start = ((bf16[2,24,2,512]{3,2,1,0:T(2,128)(2,1)}), bf16[2,24,2,512]{3,2,1,0:T(2,128)(2,1)S(1)}, u32[]{:S(2)}, u32[]{:S(2)}) async-start(bf16[2,24,2,512]{3,2,1,0:T(2,128)(2,1)} %broadcast_select_fusion.1), calls=%async_computation | async-start | bytes 196608 | tf_op jit(solution)/shard_map/all_to_all | solution.py:87
  15.2 228.5 %all-reduce.19.cloned.1.call-start = ((), (), s32[]{:S(2)}) async-start(), calls=%async_computation.2 | async-start | bytes 196608 | tf_op jit(solution)/shard_map/psum | solution.py:40
  50.0 0.7 copy-start.14
  51.6 0.7 copy-start.15
  115.8 0.8 copy-start.11
  116.9 0.7 copy-start.2
  118.2 34.1 %copy-start.4 = (bf16[512,256]{1,0:T(8,128)(2,1)S(1)}, bf16[512,256]{1,0:T(8,128)(2,1)}, u32[]{:S(2)}) copy-start(bf16[512,256]{1,0:T(8,128)(2,1)} %param.26) | copy-start | bytes 786436
  170.0 0.7 copy-start.3
  170.0 292.0 %all-reduce.17.cloned.1.call-start = ((), (), s32[]{:S(2)}) async-start(), calls=%async_computation.1 | async-start | bytes 196608 | tf_op jit(solution)/shard_map/psum | solution.py:40
  172.3 105.7 %copy-start.6 = (bf16[256,512]{1,0:T(8,128)(2,1)S(1)}, bf16[256,512]{1,0:T(8,128)(2,1)}, u32[]{:S(2)}) copy-start(bf16[256,512]{1,0:T(8,128)(2,1)} %param.28) | copy-start | bytes 786436
  243.7 34.4 %copy-start.8 = (f32[32,256]{1,0:T(8,128)S(1)}, f32[32,256]{1,0:T(8,128)}, u32[]{:S(2)}) copy-start(f32[32,256]{1,0:T(8,128)} %get-tuple-element.64) | copy-start | bytes 98308
  278.0 0.7 copy-start.13
  278.7 0.8 copy-start.9
  279.4 0.8 copy-start.10
  337.9 34.6 %copy-start.5 = (bf16[512,256]{1,0:T(8,128)(2,1)S(1)}, bf16[512,256]{1,0:T(8,128)(2,1)}, u32[]{:S(2)}) copy-start(bf16[512,256]{1,0:T(8,128)(2,1)} %param.29) | copy-start | bytes 786436
Sparse Core Ops, SparseCore 0:
  170.2 73.4 all-reduce.18
  390.8 71.1 all-reduce.16
where the time goes:
time: 471 us; the launch traced here: 470 us
  blocking collectives  286 us (61%)
  waiting for transfers between devices  142 us (30%)
  between operations  14.4 us (3%)
  local copies, waits for them, and re-layouts  10.8 us (2%)
  matrix products  7.41 us (2%)
  starting transfers between devices  5 us (1%)
  other arithmetic  4.79 us (1%)
    psum x2, waiting for transfers between devices, combine_heads(): return lax.psum(partial_out, 'tensor')  142 us
    unnamed x2, blocking collectives  120 us
    all_gather x6, blocking collectives, on_device(): context_all = lax.all_gather(context, 'enc', axis=0, tiled=True)  98 us
    psum x2, blocking collectives, row_norm(): squares = lax.psum(jnp.sum(rows_in * rows_in, axis=1), 'enc')  68.1 us
  transfers between devices with their start and end apart: 3, of which 2 were waited for; matrix products, arithmetic and copies ran while one was open for 2% of the time, Pallas kernels for 0%

commit v1 on v0

--- a/solution.py
+++ b/solution.py
@@ -8,6 +8,11 @@
 DK = 256
 STEPS = 3
 EPSILON = 1e-06
+
+
+def meshes_save(view):
+    carry_in = jnp.sum(lax.all_gather(view, "tensor"), axis=0)
+    return carry_in
 
 
 def row_norm(rows_in, gain_vec):
@@ -37,7 +42,7 @@
 
 def combine_heads(context, weight_out):
     partial_out = jnp.dot(context, weight_out, preferred_element_type=jnp.float32)
-    return lax.psum(partial_out, "tensor")
+    return meshes_save(partial_out)
 
 
 def on_device(

time: 471 us -> 519 us (1.10)
  blocking collectives: 286 us -> 496 us
  waiting for transfers between devices: 142 us -> 0.01 us
  between operations: 14.4 us -> 1.12 us
    psum x2 -> x0, waiting for transfers between devices: 142 us -> none  [combine_heads(): return lax.psum(partial_out, 'tensor')]
    all_gather x0 -> x6, blocking collectives: none -> 127 us  [meshes_save(): carry_in = jnp.sum(lax.all_gather(view, 'tensor'), axis=0)]
    unnamed x2 -> x3, blocking collectives: 120 us -> 174 us
    psum x2 -> x3, blocking collectives: 68.1 us -> 96.8 us  [row_norm(): squares = lax.psum(jnp.sum(rows_in * rows_in, axis=1), 'enc')]
  transfers between devices with their start and end apart: 3 -> 1, of which waited for: 2 -> 0; matrix products, arithmetic and copies ran while one was open for 2% -> 1% of each run, Pallas kernels for 0% -> 0%
where the time goes in v1:
time: 519 us; the launch traced here: 518 us
  blocking collectives  496 us (96%)
  local copies, waits for them, and re-layouts  8.66 us (2%)
    unnamed x3, blocking collectives  174 us
    all_gather x6, blocking collectives, meshes_save(): carry_in = jnp.sum(lax.all_gather(view, 'tensor'), axis=0)  127 us
    all_gather x6, blocking collectives, on_device(): context_all = lax.all_gather(context, 'enc', axis=0, tiled=True)  97.5 us
    psum x3, blocking collectives, row_norm(): squares = lax.psum(jnp.sum(rows_in * rows_in, axis=1), 'enc')  96.8 us
  transfers between devices with their start and end apart: 1, of which 0 were waited for; matrix products, arithmetic and copies ran while one was open for 1% of the time, Pallas kernels for 0%

profile of v1, /device:TPU:1, one launch (start us, length us, event | category | flops | bytes accessed | tf_op | source)
XLA Modules:
  0.0 517.9 jit_solution(17448926129918049210)
XLA Ops:
  0.1 0.7 copy-done.1
  0.9 0.2 fusion.89
  1.3 0.6 gather_fusion.1
  1.9 0.2 copy-done.9
  2.2 0.7 gather_fusion.3
  2.9 0.8 broadcast_select_fusion.1
  3.7 5.0 all-to-all-start
  8.8 34.7 %psum.42 = f32[32]{0:T(128)S(1)} all-reduce(f32[32]{0:T(128)S(1)} %fusion.27), channel_id=1, replica_groups=mesh['enc'=16,'dp'=2,'tensor'=4] {'enc'}, use_global_device_ids=true, to_apply=%region_1.3 | all-reduce | flops 32 | bytes 256 | tf_op jit(solution)/shard_map/psum | solution.py:19
  43.5 0.7 copy-done.11
  44.1 0.3 fusion.52
  44.4 57.1 %all-reduce.13 = bf16[32,3,512]{2,0,1:T(8,128)(2,1)S(1)} all-reduce(f32[32,3,512]{2,0,1:T(8,128)S(1)} %fusion.52), channel_id=8, replica_groups=mesh['enc'=16,'dp'=2,'tensor'=4] {'enc'}, use_global_device_ids=true, to_apply=%region_2.4.clone | all-reduce | flops 49152 | bytes 294912
  101.6 0.6 copy-done.12
  102.2 0.6 dynamic-slice.11
  103.5 0.6 copy-done.2
  104.1 0.6 gather_fusion
  105.6 15.4 %all-gather.6 = bf16[16,2,512]{2,1,0:T(2,128)(2,1)S(1)} all-gather(bf16[1,2,512]{2,1,0:T(2,128)(2,1)S(1)} %reshape.392), channel_id=1, replica_groups=mesh['enc'=16,'dp'=2,'tensor'=4] {'enc'}, dimensions={0}, use_global_device_ids=true | all-gather | bytes 34816 | tf_op jit(solution)/shard_map/all_gather | solution.py:125
  121.0 0.1 fusion.112
  121.2 32.3 %all-gather = f32[128,256]{1,0:T(8,128)S(1)} all-gather(f32[32,256]{1,0:T(8,128)S(1)} %fusion.112), channel_id=2, replica_groups=mesh['enc'=16,'dp'=2,'tensor'=4] {'tensor'}, dimensions={0}, use_global_device_ids=true | all-gather | bytes 163840 | tf_op jit(solution)/shard_map/all_gather | solution.py:14
  153.5 0.2 multiply_reduce_fusion.2
  153.6 31.0 %all-reduce.9 = (f32[32]{0:T(128)S(1)}, f32[32]{0:T(128)S(1)}) all-reduce(f32[32]{0:T(128)S(1)} %get-tuple-element.34, f32[32]{0:T(128)S(1)} %get-tuple-element.33), channel_id=1, replica_groups=mesh['enc'=16,'dp'=2,'tensor'=4] {'enc'}, use_global_device_ids=true, to_apply=%region_26.30 | all-reduce | flops 64 | bytes 512 | tf_op jit(solution)/shard_map/psum | solution.py:19
  184.7 0.3 fusion.46
  185.0 0.3 fusion.49
  185.2 59.8 %all-reduce.14 = (bf16[32,3,512]{2,0,1:T(8,128)(2,1)S(1)}, bf16[32,3,512]{2,0,1:T(8,128)(2,1)S(1)}) all-reduce(f32[32,3,512]{2,0,1:T(8,128)S(1)} %fusion.46, f32[32,3,512]{2,0,1:T(8,128)S(1)} %fusion.49), channel_id=12, replica_groups=mesh['enc'=16,'dp'=2,'tensor'=4] {'enc'}, use_global_device_ids=true, to_apply=%region_27.31.clone | all-reduce | flops 98304 | bytes 589824
  246.0 15.7 %all-gather.8 = bf16[16,2,512]{2,1,0:T(2,128)(2,1)S(1)} all-gather(bf16[1,2,512]{2,1,0:T(2,128)(2,1)S(1)} %reshape.396), channel_id=1, replica_groups=mesh['enc'=16,'dp'=2,'tensor'=4] {'enc'}, dimensions={0}, use_global_device_ids=true | all-gather | bytes 34816 | tf_op jit(solution)/shard_map/all_gather | solution.py:125
  261.8 0.1 fusion.115
  262.0 30.7 %all-gather.2 = f32[128,256]{1,0:T(8,128)S(1)} all-gather(f32[32,256]{1,0:T(8,128)S(1)} %fusion.115), channel_id=4, replica_groups=mesh['enc'=16,'dp'=2,'tensor'=4] {'tensor'}, dimensions={0}, use_global_device_ids=true | all-gather | bytes 163840 | tf_op jit(solution)/shard_map/all_gather | solution.py:14
  292.7 18.0 %all-gather.10 = bf16[16,2,512]{2,1,0:T(2,128)(2,1)S(1)} all-gather(bf16[1,2,512]{2,1,0:T(2,128)(2,1)S(1)} %reshape.400), channel_id=1, replica_groups=mesh['enc'=16,'dp'=2,'tensor'=4] {'enc'}, dimensions={0}, use_global_device_ids=true | all-gather | bytes 34816 | tf_op jit(solution)/shard_map/all_gather | solution.py:125
  310.7 0.1 fusion.118
  310.9 11.0 %all-gather.4 = f32[128,256]{1,0:T(8,128)S(1)} all-gather(f32[32,256]{1,0:T(8,128)S(1)} %fusion.118), channel_id=6, replica_groups=mesh['enc'=16,'dp'=2,'tensor'=4] {'tensor'}, dimensions={0}, use_global_device_ids=true | all-gather | bytes 163840 | tf_op jit(solution)/shard_map/all_gather | solution.py:14
  322.1 31.0 %all-reduce.7 = (f32[32]{0:T(128)S(1)}, f32[32]{0:T(128)S(1)}, f32[32]{0:T(128)S(1)}) all-reduce(f32[32]{0:T(128)S(1)} %get-tuple-element.36, f32[32]{0:T(128)S(1)} %get-tuple-element.35, f32[32]{0:T(128)S(1)} %get-tuple-element.32), channel_id=1, replica_groups=mesh['enc'=16,'dp'=2,'tensor'=4] {'enc'}, use_global_device_ids=true, to_apply=%region_34.38 | all-reduce | flops 96 | bytes 768 | tf_op jit(solution)/shard_map/psum | solution.py:19
  353.1 0.7 copy-done.10
  353.8 0.2 fusion.42
  354.0 0.2 fusion.43
  354.2 0.2 fusion.44
  354.4 57.4 %all-reduce.15 = (bf16[32,512]{1,0:T(8,128)(2,1)S(1)}, bf16[32,512]{1,0:T(8,128)(2,1)S(1)}, bf16[32,512]{1,0:T(8,128)(2,1)S(1)}) all-reduce(f32[32,512]{1,0:T(8,128)S(1)} %fusion.44, f32[32,512]{1,0:T(8,128)S(1)} %fusion.43, f32[32,512]{1,0:T(8,128)S(1)} %fusion.42), channel_id=13, replica_groups=mesh['enc'=16,'dp'=2,'tensor'=4] {'enc'}, use_global_device_ids=true, to_apply=%region_35.39.clone | all-reduce | flops 49152 | bytes 294912
  411.9 0.6 gather_fusion.2
  412.7 0.7 gather_fusion.4
  413.5 0.2 broadcast_select_fusion
  413.6 0.4 slice_reduce_fusion.1
  414.7 15.1 %all-gather.9 = bf16[16,2,512]{2,1,0:T(2,128)(2,1)S(1)} all-gather(bf16[1,2,512]{2,1,0:T(2,128)(2,1)S(1)} %reshape.398), channel_id=1, replica_groups=mesh['enc'=16,'dp'=2,'tensor'=4] {'enc'}, dimensions={0}, use_global_device_ids=true | all-gather | bytes 34816 | tf_op jit(solution)/shard_map/all_gather | solution.py:136
  430.1 31.6 %all-gather.3 = f32[128,256]{1,0:T(8,128)S(1)} all-gather(f32[32,256]{1,0:T(8,128)S(1)} %fusion.116), channel_id=5, replica_groups=mesh['enc'=16,'dp'=2,'tensor'=4] {'tensor'}, dimensions={0}, use_global_device_ids=true | all-gather | bytes 163840 | tf_op jit(solution)/shard_map/all_gather | solution.py:14
  461.9 18.0 %all-gather.11 = bf16[16,2,512]{2,1,0:T(2,128)(2,1)S(1)} all-gather(bf16[1,2,512]{2,1,0:T(2,128)(2,1)S(1)} %reshape.402), channel_id=1, replica_groups=mesh['enc'=16,'dp'=2,'tensor'=4] {'enc'}, dimensions={0}, use_global_device_ids=true | all-gather | bytes 34816 | tf_op jit(solution)/shard_map/all_gather | solution.py:136
  480.0 0.1 fusion.119
  480.1 10.9 %all-gather.5 = f32[128,256]{1,0:T(8,128)S(1)} all-gather(f32[32,256]{1,0:T(8,128)S(1)} %fusion.119), channel_id=7, replica_groups=mesh['enc'=16,'dp'=2,'tensor'=4] {'tensor'}, dimensions={0}, use_global_device_ids=true | all-gather | bytes 163840 | tf_op jit(solution)/shard_map/all_gather | solution.py:14
  491.3 15.1 %all-gather.7 = bf16[16,2,512]{2,1,0:T(2,128)(2,1)S(1)} all-gather(bf16[1,2,512]{2,1,0:T(2,128)(2,1)S(1)} %reshape.394), channel_id=1, replica_groups=mesh['enc'=16,'dp'=2,'tensor'=4] {'enc'}, dimensions={0}, use_global_device_ids=true | all-gather | bytes 34816 | tf_op jit(solution)/shard_map/all_gather | solution.py:136
  506.4 0.1 fusion.113
  506.6 10.6 %all-gather.1 = f32[128,256]{1,0:T(8,128)S(1)} all-gather(f32[32,256]{1,0:T(8,128)S(1)} %fusion.113), channel_id=3, replica_groups=mesh['enc'=16,'dp'=2,'tensor'=4] {'tensor'}, dimensions={0}, use_global_device_ids=true | all-gather | bytes 163840 | tf_op jit(solution)/shard_map/all_gather | solution.py:14
  517.2 0.6 pad_maximum_fusion
  (115 shorter events, 4.0 us)
Async XLA Ops:
  0.0 43.5 %copy-start = (bf16[256,3,512]{2,0,1:T(8,128)(2,1)S(1)}, bf16[256,3,512]{2,0,1:T(8,128)(2,1)}, u32[]{:S(2)}) copy-start(bf16[256,3,512]{2,0,1:T(8,128)(2,1)} %param.25) | copy-start | bytes 2359300
  0.1 0.7 copy-start.1
  1.3 0.9 copy-start.9
  3.7 5.0 copy-start.7
  3.7 409.0 %all-to-all-start = ((bf16[2,24,2,512]{3,2,1,0:T(2,128)(2,1)}), bf16[2,24,2,512]{3,2,1,0:T(2,128)(2,1)S(1)}, u32[]{:S(2)}, u32[]{:S(2)}) async-start(bf16[2,24,2,512]{3,2,1,0:T(2,128)(2,1)} %broadcast_select_fusion.1), calls=%async_computation | async-start | bytes 196608 | tf_op jit(solution)/shard_map/all_to_all | solution.py:92
  43.5 0.7 copy-start.11
  101.6 0.7 copy-start.12
  103.5 0.7 copy-start.2
  104.1 0.8 copy-start.8
  104.8 16.3 %copy-start.4 = (bf16[512,256]{1,0:T(8,128)(2,1)S(1)}, bf16[512,256]{1,0:T(8,128)(2,1)}, u32[]{:S(2)}) copy-start(bf16[512,256]{1,0:T(8,128)(2,1)} %param.26) | copy-start | bytes 786436
  310.9 42.2 %copy-start.6 = (bf16[256,512]{1,0:T(8,128)(2,1)S(1)}, bf16[256,512]{1,0:T(8,128)(2,1)}, u32[]{:S(2)}) copy-start(bf16[256,512]{1,0:T(8,128)(2,1)} %param.28) | copy-start | bytes 786436
  353.1 0.7 copy-start.10
  354.4 57.5 %copy-start.3 = (s32[64]{0:T(128)S(1)}, s32[64]{0:T(128)}, u32[]{:S(2)}) copy-start(s32[64]{0:T(128)} %param.22) | copy-start | bytes 772
  414.0 15.9 %copy-start.5 = (bf16[512,256]{1,0:T(8,128)(2,1)S(1)}, bf16[512,256]{1,0:T(8,128)(2,1)}, u32[]{:S(2)}) copy-start(bf16[512,256]{1,0:T(8,128)(2,1)} %param.29) | copy-start | bytes 786436
